TPU v7x, 512 devices: a whole 4x8x8 slice. The times are simulated.
512 devices in a mesh: row: 32 (over z, x), col: 16 (over y, core).
Axes of the slice: x: 4, y: 8, z: 8, core: 2. Of those that a mesh axis runs over, the one named last changes fastest.
Arguments:
- tokens: bfloat16 [16384, 5376], P('row', 'col'), may hold values from -240 to 240
- gain: float32 [5376], P('col'), may hold values from 0.1 to 1.9
- query_gain: float32 [128], replicated, may hold values from 0.1 to 1.9
- key_gain: float32 [128], replicated, may hold values from 0.1 to 1.9
- w_query: bfloat16 [5376, 4096], P('row', 'col'), may hold values from -0.21808224 to 0.21808224
- w_key: bfloat16 [5376, 2048], P('row', 'col'), may hold values from -0.21808224 to 0.21808224
- w_value: bfloat16 [5376, 2048], P('row', 'col'), may hold values from -0.21808224 to 0.21808224
Outputs:
- attended: bfloat16 [16384, 4096], P('row', 'col')
All inputs are finite; a program needn't handle non-finite values.
Results may differ from a plain program's by a relative error of at most 0.022.
Values may be sent and summed in bfloat16 or wider, within the bound.
No kernel may reach another device: no remote copies, remote signals or barrier semaphores. Data moves between devices by JAX's collectives and lax.ppermute only.
A program may use at most 64 MiB of HBM per device.

v0:
```python
import jax
import jax.numpy as jnp
from jax import lax
from jax.sharding import Mesh, PartitionSpec as P

D = 5376
HD = 128
WINDOW = 1024
EPS = 1e-06
CLIP_FRACTION = 0.25
QUERY_SCALAR = 168.0
ROPE_BASE = 10000.0
ROW = ("rz", "rx")


def shifted(array, axis, by):
    peers = lax.axis_size(axis)
    pairs = [(i, i + by) for i in range(peers) if 0 <= i + by < peers]
    return lax.ppermute(array, axis, pairs)


def ring_gather(parts, axis, dims):
    peers = lax.axis_size(axis)
    right = [(i, (i + 1) % peers) for i in range(peers)]
    left = [(i, (i - 1) % peers) for i in range(peers)]
    held = {0: parts}
    forward = parts
    backward = parts
    for step in range(1, peers // 2 + 1):
        forward = lax.ppermute(forward, axis, right)
        held[peers - step] = forward
        if step < peers - step:
            backward = lax.ppermute(backward, axis, left)
            held[step] = backward
    start = (peers - lax.axis_index(axis)) % peers
    out = []
    for leaf, dim in enumerate(dims):
        stacked = jnp.concatenate([held[k][leaf] for k in range(peers)], axis=dim)
        doubled = jnp.concatenate([stacked, stacked], axis=dim)
        size = parts[leaf].shape[dim]
        out.append(lax.dynamic_slice_in_dim(doubled, start * size, peers * size, dim))
    return tuple(out)


def clip_with(weight, largest):
    bound = CLIP_FRACTION * largest
    return jnp.clip(weight.astype(jnp.float32), -bound, bound).astype(jnp.bfloat16)


def column_max(weight):
    return jnp.max(jnp.abs(weight.astype(jnp.float32)), axis=0)


def head_norm(values, head_gain):
    return values * lax.rsqrt(jnp.mean(values * values, axis=-1, keepdims=True) + EPS) * head_gain


def rotate(values, positions):
    half = values.shape[-1] // 2
    freqs = ROPE_BASE ** (-(jnp.arange(half, dtype=jnp.float32) * 2.0 / values.shape[-1]))
    angles = positions.astype(jnp.float32)[:, None] * freqs[None, :]
    cosine = jnp.cos(angles)[:, None, :]
    sine = jnp.sin(angles)[:, None, :]
    first = values[..., :half]
    second = values[..., half:]
    return jnp.concatenate(
        [first * cosine - second * sine, second * cosine + first * sine], axis=-1
    )


def local(tokens, gain, query_gain, key_gain, w_query, w_key, w_value):
    rows = tokens.shape[0]
    query_cols = w_query.shape[1]
    key_cols = w_key.shape[1]
    stacked = jnp.concatenate([w_query, w_key, w_value], axis=1)
    weight_rows, weight_cols = stacked.shape
    aligned = -(-(weight_rows + 1) // TILE_ROWS) * TILE_ROWS
    local_max = jnp.max(jnp.abs(stacked), axis=0)
    padded = jnp.concatenate(
        [
            stacked,
            local_max[None],
            jnp.zeros((aligned - weight_rows - 1, weight_cols), stacked.dtype),
        ],
        axis=0,
    )
    slabs = lax.all_gather(padded, ROW, axis=0, tiled=True).reshape(-1, aligned, weight_cols)
    largest = jnp.max(slabs[:, weight_rows].astype(jnp.float32), axis=0)

    def clipped_columns(first, last):
        part = slabs[:, :weight_rows, first:last].reshape(-1, last - first)
        return clip_with(part, largest[first:last])

    rows_tokens, piece = tokens.shape
    cores = lax.axis_size("cc")
    high = gain.astype(jnp.bfloat16)
    rest = gain - high.astype(jnp.float32)
    middle = rest.astype(jnp.bfloat16)
    low = (rest - middle.astype(jnp.float32)).astype(jnp.bfloat16)
    filler = jnp.zeros((GAIN_ROWS - 3, piece), jnp.bfloat16)
    packed = jnp.concatenate([tokens, high[None], middle[None], low[None], filler], axis=0)
    (along_y,) = ring_gather((packed,), "cy", (1,))
    (along_all,) = ring_gather((along_y,), "cc", (1,))
    blocks = along_all.shape[1] // (cores * piece)
    split = along_all[rows_tokens : rows_tokens + 3].astype(jnp.float32)
    full_gain = split[0] + (split[1] + split[2])
    widened = along_all[:rows_tokens].astype(jnp.float32)
    squares = jnp.sum(widened * widened, axis=1)
    inverse = lax.rsqrt(squares / D + EPS)[:, None]
    whole = (widened * inverse * full_gain[None, :]).astype(jnp.bfloat16)

    def ordered(first, last):
        part = clipped_columns(first, last)
        return (
            part.reshape(blocks, cores, piece, last - first)
            .transpose(1, 0, 2, 3)
            .reshape(part.shape)
        )

    kv_part = jnp.dot(whole, ordered(query_cols, weight_cols), preferred_element_type=jnp.float32)
    keys = kv_part[:, :key_cols]
    values = kv_part[:, key_cols:]
    query = jnp.dot(whole, ordered(0, query_cols), preferred_element_type=jnp.float32)
    heads_local = query_cols // HD
    kv_local = key_cols // HD
    group = heads_local // kv_local
    positions = lax.axis_index(ROW) * rows + jnp.arange(rows, dtype=jnp.int32)
    query = rotate(head_norm(query.reshape(rows, heads_local, HD), query_gain), positions).astype(
        jnp.bfloat16
    )
    keys = rotate(head_norm(keys.reshape(rows, kv_local, HD), key_gain), positions).astype(
        jnp.bfloat16
    )
    values = values.reshape(rows, kv_local, HD).astype(jnp.bfloat16)
    blocks_back = WINDOW // rows
    both = jnp.concatenate([keys, values], axis=1)
    earlier = [shifted(both, ROW, offset) for offset in range(blocks_back, 0, -1)]
    joined = jnp.concatenate(earlier + [both], axis=0)
    all_keys = joined[:, :kv_local]
    all_values = joined[:, kv_local:]
    key_pos = (
        positions[0] - blocks_back * rows + jnp.arange((blocks_back + 1) * rows, dtype=jnp.int32)
    )
    grouped = query.reshape(rows, kv_local, group, HD)
    scores = jnp.einsum(
        "tkgd,skd->kgts", grouped, all_keys, preferred_element_type=jnp.float32
    ) * QUERY_SCALAR ** (-0.5)
    distance = positions[:, None] - key_pos[None, :]
    allowed = (distance >= 0) & (distance < WINDOW) & (key_pos[None, :] >= 0)
    expo = jnp.where(allowed, jnp.exp(scores), 0.0)
    total = jnp.sum(expo, axis=-1, keepdims=True)
    probs = (expo / total).astype(jnp.bfloat16)
    output = jnp.einsum("kgts,skd->tkgd", probs, all_values, preferred_element_type=jnp.float32)
    return output.reshape(rows, query_cols).astype(jnp.bfloat16)


CORES_PER_CHIP = 2
GAIN_ROWS = 8
TILE_ROWS = 16


def solution(mesh):
    rows, cols = (mesh.shape["row"], mesh.shape["col"])
    minor = len({tuple(getattr(d, "coords", (0,)))[0] for d in mesh.devices[:, 0].flat})
    if rows % minor:
        minor = 1
    split = Mesh(
        mesh.devices.reshape(rows // minor, minor, cols // CORES_PER_CHIP, CORES_PER_CHIP),
        ("rz", "rx", "cy", "cc"),
    )
    col = ("cy", "cc")
    placed = (P(ROW, col), P(col), P(), P(), P(ROW, col), P(ROW, col), P(ROW, col))
    return jax.shard_map(local, mesh=split, in_specs=placed, out_specs=P(ROW, col), check_vma=False)
```

profile of v0, /device:TPU:8, one launch (start us, length us, event | category | flops | bytes accessed | tf_op | source)
XLA Modules:
  0.0 144.5 jit_solution(14223948098695784840)
XLA Ops:
  12.2 3.5 %collective-permute-start.3 = (bf16[520,336]{1,0:T(8,128)(2,1)S(1)}, bf16[520,336]{1,0:T(8,128)(2,1)S(1)}, u32[]{:S(2)}, u32[]{:S(2)}) collective-permute-start(bf16[520,336]{1,0:T(8,128)(2,1)S(1)} %concatenate.43), channel_id=1, source_target_pairs={{0,2},{2,4},{4,6},{6,8},{8,10},{10,12},{12,14},{14,0},{1,3},{3,5},... | collective-permute-start | bytes 1048328 | tf_op jit(solution)/shard_map/ppermute | solution.py:30
  15.7 6.2 %collective-permute-start = (bf16[520,336]{1,0:T(8,128)(2,1)S(1)}, bf16[520,336]{1,0:T(8,128)(2,1)S(1)}, u32[]{:S(2)}, u32[]{:S(2)}) collective-permute-start(bf16[520,336]{1,0:T(8,128)(2,1)S(1)} %concatenate.43), channel_id=1, source_target_pairs={{0,14},{2,0},{4,2},{6,4},{8,6},{10,8},{12,10},{14,12},{1,15},{3,1}... | collective-permute-start | bytes 1048328 | tf_op jit(solution)/shard_map/ppermute | solution.py:33
  21.9 3.9 %collective-permute-done.3 = bf16[520,336]{1,0:T(8,128)(2,1)S(1)} collective-permute-done((bf16[520,336]{1,0:T(8,128)(2,1)S(1)}, bf16[520,336]{1,0:T(8,128)(2,1)S(1)}, u32[]{:S(2)}, u32[]{:S(2)}) %collective-permute-start.3) | collective-permute-done | bytes 349472 | tf_op jit(solution)/shard_map/ppermute | solution.py:30
  25.8 2.8 %collective-permute-start.4 = (bf16[520,336]{1,0:T(8,128)(2,1)S(1)}, bf16[520,336]{1,0:T(8,128)(2,1)S(1)}, u32[]{:S(2)}, u32[]{:S(2)}) collective-permute-start(bf16[520,336]{1,0:T(8,128)(2,1)S(1)} %collective-permute-done.3), channel_id=1, source_target_pairs={{0,2},{2,4},{4,6},{6,8},{8,10},{10,12},{12,14},{14,0},{1,3},{3,5},... | collective-permute-start | bytes 1048328 | tf_op jit(solution)/shard_map/ppermute | solution.py:30
  28.6 4.2 %collective-permute-start.1 = (bf16[520,336]{1,0:T(8,128)(2,1)S(1)}, bf16[520,336]{1,0:T(8,128)(2,1)S(1)}, u32[]{:S(2)}, u32[]{:S(2)}) collective-permute-start(bf16[520,336]{1,0:T(8,128)(2,1)S(1)} %collective-permute-done), channel_id=1, source_target_pairs={{0,14},{2,0},{4,2},{6,4},{8,6},{10,8},{12,10},{14,12},{1,15},{3,1}... | collective-permute-start | bytes 1048328 | tf_op jit(solution)/shard_map/ppermute | solution.py:33
  32.8 3.9 %collective-permute-done.4 = bf16[520,336]{1,0:T(8,128)(2,1)S(1)} collective-permute-done((bf16[520,336]{1,0:T(8,128)(2,1)S(1)}, bf16[520,336]{1,0:T(8,128)(2,1)S(1)}, u32[]{:S(2)}, u32[]{:S(2)}) %collective-permute-start.4) | collective-permute-done | bytes 349472 | tf_op jit(solution)/shard_map/ppermute | solution.py:30
  36.7 3.9 %collective-permute-start.5 = (bf16[520,336]{1,0:T(8,128)(2,1)S(1)}, bf16[520,336]{1,0:T(8,128)(2,1)S(1)}, u32[]{:S(2)}, u32[]{:S(2)}) collective-permute-start(bf16[520,336]{1,0:T(8,128)(2,1)S(1)} %collective-permute-done.4), channel_id=1, source_target_pairs={{0,2},{2,4},{4,6},{6,8},{8,10},{10,12},{12,14},{14,0},{1,3},{3,5},... | collective-permute-start | bytes 1048328 | tf_op jit(solution)/shard_map/ppermute | solution.py:30
  41.2 2.6 %collective-permute-start.2 = (bf16[520,336]{1,0:T(8,128)(2,1)S(1)}, bf16[520,336]{1,0:T(8,128)(2,1)S(1)}, u32[]{:S(2)}, u32[]{:S(2)}) collective-permute-start(bf16[520,336]{1,0:T(8,128)(2,1)S(1)} %collective-permute-done.1), channel_id=1, source_target_pairs={{0,14},{2,0},{4,2},{6,4},{8,6},{10,8},{12,10},{14,12},{1,15},{3,1}... | collective-permute-start | bytes 1048328 | tf_op jit(solution)/shard_map/ppermute | solution.py:33
  43.8 3.9 %collective-permute-done.5 = bf16[520,336]{1,0:T(8,128)(2,1)S(1)} collective-permute-done((bf16[520,336]{1,0:T(8,128)(2,1)S(1)}, bf16[520,336]{1,0:T(8,128)(2,1)S(1)}, u32[]{:S(2)}, u32[]{:S(2)}) %collective-permute-start.5) | collective-permute-done | bytes 349472 | tf_op jit(solution)/shard_map/ppermute | solution.py:30
  47.6 4.6 %collective-permute-start.6 = (bf16[520,336]{1,0:T(8,128)(2,1)S(1)}, bf16[520,336]{1,0:T(8,128)(2,1)S(1)}, u32[]{:S(2)}, u32[]{:S(2)}) collective-permute-start(bf16[520,336]{1,0:T(8,128)(2,1)S(1)} %collective-permute-done.5), channel_id=1, source_target_pairs={{0,2},{2,4},{4,6},{6,8},{8,10},{10,12},{12,14},{14,0},{1,3},{3,5},... | collective-permute-start | bytes 1048328 | tf_op jit(solution)/shard_map/ppermute | solution.py:30
  53.6 5.0 %collective-permute-done.6 = bf16[520,336]{1,0:T(8,128)(2,1)S(1)} collective-permute-done((bf16[520,336]{1,0:T(8,128)(2,1)S(1)}, bf16[520,336]{1,0:T(8,128)(2,1)S(1)}, u32[]{:S(2)}, u32[]{:S(2)}) %collective-permute-start.6) | collective-permute-done | bytes 349472 | tf_op jit(solution)/shard_map/ppermute | solution.py:30
  58.6 7.6 %concatenate.44 = bf16[520,5376]{1,0:T(8,128)(2,1)} concatenate(bf16[520,336]{1,0:T(8,128)(2,1)S(1)} %concatenate.43, bf16[520,336]{1,0:T(8,128)(2,1)S(1)} %collective-permute-done, bf16[520,336]{1,0:T(8,128)(2,1)S(1)} %collective-permute-done.1, bf16[520,336]{1,0:T(8,128)(2,1)S(1)} %collective-permute-done.2, bf16[520,336]{1,0:T(8,128)(2,1)S(1)} %collective-permute-done.6, ...), dimensions={1} | concatenate | bytes 11182080 | tf_op jit(solution)/shard_map/concatenate | solution.py:39
  66.2 3.3 %constant_dynamic-slice_fusion = bf16[520,2688]{1,0:T(8,128)(2,1)S(1)} fusion(bf16[520,5376]{1,0:T(8,128)(2,1)} %concatenate.44, s32[]{:T(128)S(6)} %select_n.22), kind=kLoop, calls=%fused_computation.80 | loop fusion | bytes 5591044 | tf_op jit(solution)/shard_map/dynamic_slice | solution.py:41
  69.5 2.1 %collective-permute-start.7 = (bf16[520,2688]{1,0:T(8,128)(2,1)S(1)}, bf16[520,2688]{1,0:T(8,128)(2,1)}, u32[]{:S(2)}, u32[]{:S(2)}) collective-permute-start(bf16[520,2688]{1,0:T(8,128)(2,1)S(1)} %constant_dynamic-slice_fusion), channel_id=1, source_target_pairs={{0,1},{1,0},{2,3},{3,2},{4,5},{5,4},{6,7},{7,6},{8,9},{9,8},{10,11... | collective-permute-start | bytes 8386568 | tf_op jit(solution)/shard_map/ppermute | solution.py:30
  76.7 5.2 %fusion.5 = bf16[520,5376]{1,0:T(8,128)(2,1)S(1)} fusion(s32[]{:T(128)S(6)} %select_n.24, bf16[520,2688]{1,0:T(8,128)(2,1)S(1)} %constant_dynamic-slice_fusion, bf16[520,2688]{1,0:T(8,128)(2,1)} %collective-permute-done.7), kind=kLoop, calls=%fused_computation.13 | loop fusion | flops 22364160 | bytes 11182084 | tf_op jit(solution)/shard_map/concatenate | solution.py:39
  82.0 2.4 %copy-done = bf16[520,5376]{1,0:T(8,128)(2,1)} copy-done((bf16[520,5376]{1,0:T(8,128)(2,1)}, bf16[520,5376]{1,0:T(8,128)(2,1)S(1)}, u32[]{:S(2)}) %copy-start) | copy-done | bytes 5591064
  85.5 22.3 %all-gather.2.cloned.1.call-done = bf16[5632,512]{1,0:T(8,128)(2,1)} async-done(((bf16[176,512]{1,0:T(8,128)(2,1)}), bf16[5632,512]{1,0:T(8,128)(2,1)}) %all-gather.2.cloned.1.call-update) | async-done | bytes 5767184 | tf_op jit(solution)/shard_map/all_gather | solution.py:87
  108.9 3.2 %fusion.47 = (bf16[32,168,256]{2,1,0:T(8,128)(2,1)S(1)}, bf16[32,168,256]{2,1,0:T(8,128)(2,1)S(1)}) fusion(bf16[32,176,512]{2,1,0:T(8,128)(2,1)} %bitcast.66), kind=kLoop, calls=%fused_computation.90 | loop fusion | bytes 11010048 | tf_op jit(solution)/shard_map/slice | solution.py:91
  113.6 2.0 %fusion.23 = f32[512,256]{0,1:T(8,128)S(1)} fusion(bf16[5376,256]{1,0:T(8,128)(2,1)S(1)} %bitcast.68, f32[5376]{0:T(1024)S(1)} %fusion.39, f32[512]{0:T(512)S(1)} %add_rsqrt_fusion.2, bf16[520,5376]{1,0:T(8,128)(2,1)S(1)} %bitcast.61), kind=kOutput, calls=%fused_computation.32 | convolution fusion | flops 1420296192 | bytes 8808448 | tf_op jit(solution)/shard_map/dot_general | solution.py:120
  116.4 4.1 %collective-permute-start.8 = (bf16[512,2,128]{0,2,1:T(8,128)(2,1)S(1)}, bf16[512,2,128]{0,2,1:T(8,128)(2,1)}, u32[]{:S(2)}, u32[]{:S(2)}) collective-permute-start(bf16[512,2,128]{0,2,1:T(8,128)(2,1)S(1)} %pad_maximum_fusion), channel_id=1, source_target_pairs={{0,32},{16,48},{32,64},{48,80},{64,96},{80,112},{96,128},{112,144}... | collective-permute-start | bytes 786440 | tf_op jit(solution)/shard_map/ppermute | solution.py:19
  120.4 2.9 %collective-permute-start.9 = (bf16[512,2,128]{0,2,1:T(8,128)(2,1)S(1)}, bf16[512,2,128]{0,2,1:T(8,128)(2,1)}, u32[]{:S(2)}, u32[]{:S(2)}) collective-permute-start(bf16[512,2,128]{0,2,1:T(8,128)(2,1)S(1)} %pad_maximum_fusion), channel_id=1, source_target_pairs={{0,16},{16,32},{32,48},{48,64},{64,80},{80,96},{96,112},{112,128},... | collective-permute-start | bytes 786440 | tf_op jit(solution)/shard_map/ppermute | solution.py:19
  123.5 3.0 %copy.46 = bf16[256,5376]{1,0:T(8,128)(2,1)} copy(bf16[256,5376]{0,1:T(8,128)(2,1)S(1)} %bitcast.64) | data formatting | bytes 5505024 | tf_op jit(solution)/shard_map/dot_general | solution.py:123
  126.5 5.2 %multiply_reduce_fusion = (f32[512,2]{0,1:T(2,128)S(1)}, f32[512,2,128]{0,2,1:T(8,128)S(1)}) fusion(bf16[2,128,5376]{2,1,0:T(8,128)(2,1)} %bitcast.67, f32[5376]{0:T(1024)} %copy-done.2, f32[512]{0:T(512)S(1)} %add_rsqrt_fusion.2, bf16[520,5376]{1,0:T(8,128)(2,1)} %copy-done), kind=kOutput, calls=%fused_computation.35 | convolution fusion | flops 1420557312 | bytes 8812544 | tf_op jit(solution)/shard_map/dot_general | solution.py:123
  134.8 2.0 %fusion.19 = bf16[128,2,512]{2,0,1:T(8,128)(2,1)S(1)} fusion(f32[2,512]{1,0:T(2,128)S(1)} %get-tuple-element.22, f32[1536,512,2]{1,0,2:T(8,128)S(1)} %get-tuple-element.23, pred[512,1536]{0,1:T(8,128)(4,1)S(1)} %copy-done.1, bf16[1536,2,128]{0,2,1:T(8,128)(2,1)S(1)} %maximum_maximum_fusion), kind=kOutput, calls=%fused_computation.31 | convolution fusion | flops 409075712 | bytes 7737344 | tf_op jit(solution)/shard_map/kgts,skd->tkgd/dot_general | solution.py:153
  (67 shorter events, 20.5 us)
Async XLA Ops:
  6.5 101.3 %all-gather.2.cloned.1.call-start = ((), (), s32[]{:S(2)}) async-start(), calls=%async_computation | async-start | bytes 5947392 | tf_op jit(solution)/shard_map/all_gather | solution.py:87
  12.2 13.5 %collective-permute-start.3 = (bf16[520,336]{1,0:T(8,128)(2,1)S(1)}, bf16[520,336]{1,0:T(8,128)(2,1)S(1)}, u32[]{:S(2)}, u32[]{:S(2)}) collective-permute-start(bf16[520,336]{1,0:T(8,128)(2,1)S(1)} %concatenate.43), channel_id=1, source_target_pairs={{0,2},{2,4},{4,6},{6,8},{8,10},{10,12},{12,14},{14,0},{1,3},{3,5},... | collective-permute-start | bytes 1048328 | tf_op jit(solution)/shard_map/ppermute | solution.py:30
  15.7 12.9 %collective-permute-start = (bf16[520,336]{1,0:T(8,128)(2,1)S(1)}, bf16[520,336]{1,0:T(8,128)(2,1)S(1)}, u32[]{:S(2)}, u32[]{:S(2)}) collective-permute-start(bf16[520,336]{1,0:T(8,128)(2,1)S(1)} %concatenate.43), channel_id=1, source_target_pairs={{0,14},{2,0},{4,2},{6,4},{8,6},{10,8},{12,10},{14,12},{1,15},{3,1}... | collective-permute-start | bytes 1048328 | tf_op jit(solution)/shard_map/ppermute | solution.py:33
  25.8 10.9 %collective-permute-start.4 = (bf16[520,336]{1,0:T(8,128)(2,1)S(1)}, bf16[520,336]{1,0:T(8,128)(2,1)S(1)}, u32[]{:S(2)}, u32[]{:S(2)}) collective-permute-start(bf16[520,336]{1,0:T(8,128)(2,1)S(1)} %collective-permute-done.3), channel_id=1, source_target_pairs={{0,2},{2,4},{4,6},{6,8},{8,10},{10,12},{12,14},{14,0},{1,3},{3,5},... | collective-permute-start | bytes 1048328 | tf_op jit(solution)/shard_map/ppermute | solution.py:30
  28.6 12.6 %collective-permute-start.1 = (bf16[520,336]{1,0:T(8,128)(2,1)S(1)}, bf16[520,336]{1,0:T(8,128)(2,1)S(1)}, u32[]{:S(2)}, u32[]{:S(2)}) collective-permute-start(bf16[520,336]{1,0:T(8,128)(2,1)S(1)} %collective-permute-done), channel_id=1, source_target_pairs={{0,14},{2,0},{4,2},{6,4},{8,6},{10,8},{12,10},{14,12},{1,15},{3,1}... | collective-permute-start | bytes 1048328 | tf_op jit(solution)/shard_map/ppermute | solution.py:33
  36.7 10.9 %collective-permute-start.5 = (bf16[520,336]{1,0:T(8,128)(2,1)S(1)}, bf16[520,336]{1,0:T(8,128)(2,1)S(1)}, u32[]{:S(2)}, u32[]{:S(2)}) collective-permute-start(bf16[520,336]{1,0:T(8,128)(2,1)S(1)} %collective-permute-done.4), channel_id=1, source_target_pairs={{0,2},{2,4},{4,6},{6,8},{8,10},{10,12},{12,14},{14,0},{1,3},{3,5},... | collective-permute-start | bytes 1048328 | tf_op jit(solution)/shard_map/ppermute | solution.py:30
  41.2 12.4 %collective-permute-start.2 = (bf16[520,336]{1,0:T(8,128)(2,1)S(1)}, bf16[520,336]{1,0:T(8,128)(2,1)S(1)}, u32[]{:S(2)}, u32[]{:S(2)}) collective-permute-start(bf16[520,336]{1,0:T(8,128)(2,1)S(1)} %collective-permute-done.1), channel_id=1, source_target_pairs={{0,14},{2,0},{4,2},{6,4},{8,6},{10,8},{12,10},{14,12},{1,15},{3,1}... | collective-permute-start | bytes 1048328 | tf_op jit(solution)/shard_map/ppermute | solution.py:33
  47.6 10.9 %collective-permute-start.6 = (bf16[520,336]{1,0:T(8,128)(2,1)S(1)}, bf16[520,336]{1,0:T(8,128)(2,1)S(1)}, u32[]{:S(2)}, u32[]{:S(2)}) collective-permute-start(bf16[520,336]{1,0:T(8,128)(2,1)S(1)} %collective-permute-done.5), channel_id=1, source_target_pairs={{0,2},{2,4},{4,6},{6,8},{8,10},{10,12},{12,14},{14,0},{1,3},{3,5},... | collective-permute-start | bytes 1048328 | tf_op jit(solution)/shard_map/ppermute | solution.py:30
  69.5 7.2 %collective-permute-start.7 = (bf16[520,2688]{1,0:T(8,128)(2,1)S(1)}, bf16[520,2688]{1,0:T(8,128)(2,1)}, u32[]{:S(2)}, u32[]{:S(2)}) collective-permute-start(bf16[520,2688]{1,0:T(8,128)(2,1)S(1)} %constant_dynamic-slice_fusion), channel_id=1, source_target_pairs={{0,1},{1,0},{2,3},{3,2},{4,5},{5,4},{6,7},{7,6},{8,9},{9,8},{10,11... | collective-permute-start | bytes 8386568 | tf_op jit(solution)/shard_map/ppermute | solution.py:30
  81.8 2.5 %copy-start = (bf16[520,5376]{1,0:T(8,128)(2,1)}, bf16[520,5376]{1,0:T(8,128)(2,1)S(1)}, u32[]{:S(2)}) copy-start(bf16[520,5376]{1,0:T(8,128)(2,1)S(1)} %fusion.5) | copy-start | bytes 16773124
  84.3 29.2 %copy-start.2 = (f32[5376]{0:T(1024)}, f32[5376]{0:T(1024)S(1)}, u32[]{:S(2)}) copy-start(f32[5376]{0:T(1024)S(1)} %fusion.39) | copy-start | bytes 64516
  108.9 4.7 %slice-start = ((s8[5591040]{0:T(1024)(128)(4,1)}), s8[4194304]{0:T(1024)(128)(4,1)S(1)}, s32[]{:S(2)}) async-start(s8[5591040]{0:T(1024)(128)(4,1)} %bitcast.60), calls=%async_computation.1 | async-start | bytes 8388608
  112.1 1.5 %slice-start.1 = ((s8[5591040]{0:T(1024)(128)(4,1)}), s8[1396736]{0:T(1024)(128)(4,1)S(1)}, s32[]{:S(2)}) async-start(s8[5591040]{0:T(1024)(128)(4,1)} %bitcast.60), calls=%async_computation.2 | async-start | bytes 2793472
  113.6 2.1 %copy-start.3 = (f32[128]{0:T(128)S(1)}, f32[128]{0:T(128)}, u32[]{:S(2)}) copy-start(f32[128]{0:T(128)} %param.10) | copy-start | bytes 1540
  116.4 15.6 %collective-permute-start.8 = (bf16[512,2,128]{0,2,1:T(8,128)(2,1)S(1)}, bf16[512,2,128]{0,2,1:T(8,128)(2,1)}, u32[]{:S(2)}, u32[]{:S(2)}) collective-permute-start(bf16[512,2,128]{0,2,1:T(8,128)(2,1)S(1)} %pad_maximum_fusion), channel_id=1, source_target_pairs={{0,32},{16,48},{32,64},{48,80},{64,96},{80,112},{96,128},{112,144}... | collective-permute-start | bytes 786440 | tf_op jit(solution)/shard_map/ppermute | solution.py:19
  120.4 11.5 %collective-permute-start.9 = (bf16[512,2,128]{0,2,1:T(8,128)(2,1)S(1)}, bf16[512,2,128]{0,2,1:T(8,128)(2,1)}, u32[]{:S(2)}, u32[]{:S(2)}) collective-permute-start(bf16[512,2,128]{0,2,1:T(8,128)(2,1)S(1)} %pad_maximum_fusion), channel_id=1, source_target_pairs={{0,16},{16,32},{32,48},{48,64},{64,80},{80,96},{96,112},{112,128},... | collective-permute-start | bytes 786440 | tf_op jit(solution)/shard_map/ppermute | solution.py:19
  126.5 5.2 %copy-start.4 = (f32[128]{0:T(128)S(1)}, f32[128]{0:T(128)}, u32[]{:S(2)}) copy-start(f32[128]{0:T(128)} %param.9) | copy-start | bytes 1540
  126.5 6.5 %copy-start.1 = (pred[512,1536]{0,1:T(8,128)(4,1)S(1)}, pred[512,1536]{0,1:T(8,128)(4,1)}, u32[]{:S(2)}) copy-start(pred[512,1536]{0,1:T(8,128)(4,1)} %fusion.16) | copy-start | bytes 2359300
Sparse Core Ops, SparseCore 0:
  10.5 97.2 all-gather.1
where the time goes:
time: 145 us; the launch traced here: 144 us
  waiting for transfers between devices  42.1 us (29%)
  starting transfers between devices  36.8 us (25%)
  local copies, waits for them, and re-layouts  25.3 us (17%)
  other arithmetic  14.9 us (10%)
  between operations  14.5 us (10%)
  matrix products  10.9 us (8%)
    all_gather x1, waiting for transfers between devices, local(): lax.all_gather(padded, ROW, axis=0, tiled=True)  22.3 us
    ppermute x5, waiting for transfers between devices, ring_gather(): forward = lax.ppermute(forward, axis, right)  17.8 us
    ppermute x5, starting transfers between devices, ring_gather(): forward = lax.ppermute(forward, axis, right)  16.9 us
    ppermute x3, starting transfers between devices, ring_gather(): backward = lax.ppermute(backward, axis, left)  13 us
    concatenate x1, local copies, waits for them, and re-layouts, ring_gather(): doubled = jnp.concatenate([stacked, stacked], axis=dim)  7.61 us
    ppermute x2, starting transfers between devices, shifted(): return lax.ppermute(array, axis, pairs)  6.96 us
    unnamed x17, local copies, waits for them, and re-layouts  5.32 us
    dot_general x1, matrix products, local(): jnp.dot(whole, ordered(0, query_cols), preferred_element_type=jnp.float32)  5.2 us
  transfers between devices with their start and end apart: 11, of which 8 were waited for; matrix products, arithmetic and copies ran while one was open for 22% of the time, Pallas kernels for 0%

commit v1 on v0

--- a/solution.py
+++ b/solution.py
@@ -84,7 +84,9 @@
         ],
         axis=0,
     )
-    slabs = lax.all_gather(padded, ROW, axis=0, tiled=True).reshape(-1, aligned, weight_cols)
+    slabs = jnp.concatenate(
+        lax.all_to_all(jnp.stack([padded] * lax.axis_size(ROW)), ROW, 0, 0), axis=0
+    ).reshape(-1, aligned, weight_cols)
     largest = jnp.max(slabs[:, weight_rows].astype(jnp.float32), axis=0)
 
     def clipped_columns(first, last):

time: 145 us -> 184 us (1.27)
  the two profiles are of different devices: /device:TPU:8 before, /device:TPU:1 now
where the time goes in v1:
time: 184 us; the launch traced here: 183 us
  waiting for transfers between devices  74.6 us (41%)
  starting transfers between devices  55.6 us (30%)
  local copies, waits for them, and re-layouts  27.3 us (15%)
  other arithmetic  13.4 us (7%)
  matrix products  10.9 us (6%)
    all_to_all x1, waiting for transfers between devices, local(): lax.all_to_all(jnp.stack([padded] * lax.axis_size(ROW)), ROW, 0, 0)  46.8 us
    ppermute x5, waiting for transfers between devices, ring_gather(): forward = lax.ppermute(forward, axis, right)  27.8 us
    ppermute x5, starting transfers between devices, ring_gather(): forward = lax.ppermute(forward, axis, right)  14.9 us
    all_to_all x1, starting transfers between devices, local(): lax.all_to_all(jnp.stack([padded] * lax.axis_size(ROW)), ROW, 0, 0)  14 us
    ppermute x2, starting transfers between devices, shifted(): return lax.ppermute(array, axis, pairs)  13.7 us
    ppermute x3, starting transfers between devices, ring_gather(): backward = lax.ppermute(backward, axis, left)  13 us
    concatenate x1, local copies, waits for them, and re-layouts, ring_gather(): doubled = jnp.concatenate([stacked, stacked], axis=dim)  7.59 us
    dot_general x1, matrix products, local(): jnp.dot(whole, ordered(0, query_cols), preferred_element_type=jnp.float32)  5.2 us
  transfers between devices with their start and end apart: 11, of which 6 were waited for; matrix products, arithmetic and copies ran while one was open for 16% of the time, Pallas kernels for 0%

profile of v1, /device:TPU:1, one launch (start us, length us, event | category | flops | bytes accessed | tf_op | source)
XLA Modules:
  0.0 182.9 jit_solution(8257374237342944789)
XLA Ops:
  2.7 3.1 %stack.2 = bf16[32,176,512]{2,1,0:T(8,128)(2,1)} broadcast(bf16[176,512]{1,0:T(8,128)(2,1)S(1)} %maximum_maximum_fusion.1), dimensions={1,2} | broadcast | bytes 5947392 | tf_op jit(solution)/shard_map/stack | solution.py:88
  5.9 14.0 %all-to-all-start = ((bf16[32,176,512]{2,1,0:T(8,128)(2,1)}), bf16[32,176,512]{2,1,0:T(8,128)(2,1)}, u32[]{:S(2)}, u32[]{:S(2)}) async-start(bf16[32,176,512]{2,1,0:T(8,128)(2,1)} %stack.2), calls=%async_computation | async-start | bytes 11534336 | tf_op jit(solution)/shard_map/all_to_all | solution.py:88
  20.4 3.2 %collective-permute-start.3 = (bf16[520,336]{1,0:T(8,128)(2,1)S(1)}, bf16[520,336]{1,0:T(8,128)(2,1)S(1)}, u32[]{:S(2)}, u32[]{:S(2)}) collective-permute-start(bf16[520,336]{1,0:T(8,128)(2,1)S(1)} %concatenate.43), channel_id=1, source_target_pairs={{0,2},{2,4},{4,6},{6,8},{8,10},{10,12},{12,14},{14,0},{1,3},{3,5},... | collective-permute-start | bytes 1048328 | tf_op jit(solution)/shard_map/ppermute | solution.py:30
  23.6 3.8 %collective-permute-start = (bf16[520,336]{1,0:T(8,128)(2,1)S(1)}, bf16[520,336]{1,0:T(8,128)(2,1)S(1)}, u32[]{:S(2)}, u32[]{:S(2)}) collective-permute-start(bf16[520,336]{1,0:T(8,128)(2,1)S(1)} %concatenate.43), channel_id=1, source_target_pairs={{0,14},{2,0},{4,2},{6,4},{8,6},{10,8},{12,10},{14,12},{1,15},{3,1}... | collective-permute-start | bytes 1048328 | tf_op jit(solution)/shard_map/ppermute | solution.py:33
  27.4 6.8 %collective-permute-done.3 = bf16[520,336]{1,0:T(8,128)(2,1)S(1)} collective-permute-done((bf16[520,336]{1,0:T(8,128)(2,1)S(1)}, bf16[520,336]{1,0:T(8,128)(2,1)S(1)}, u32[]{:S(2)}, u32[]{:S(2)}) %collective-permute-start.3) | collective-permute-done | bytes 349472 | tf_op jit(solution)/shard_map/ppermute | solution.py:30
  36.2 4.6 %collective-permute-start.1 = (bf16[520,336]{1,0:T(8,128)(2,1)S(1)}, bf16[520,336]{1,0:T(8,128)(2,1)S(1)}, u32[]{:S(2)}, u32[]{:S(2)}) collective-permute-start(bf16[520,336]{1,0:T(8,128)(2,1)S(1)} %collective-permute-done), channel_id=1, source_target_pairs={{0,14},{2,0},{4,2},{6,4},{8,6},{10,8},{12,10},{14,12},{1,15},{3,1}... | collective-permute-start | bytes 1048328 | tf_op jit(solution)/shard_map/ppermute | solution.py:33
  40.7 6.0 %collective-permute-done.4 = bf16[520,336]{1,0:T(8,128)(2,1)S(1)} collective-permute-done((bf16[520,336]{1,0:T(8,128)(2,1)S(1)}, bf16[520,336]{1,0:T(8,128)(2,1)S(1)}, u32[]{:S(2)}, u32[]{:S(2)}) %collective-permute-start.4) | collective-permute-done | bytes 349472 | tf_op jit(solution)/shard_map/ppermute | solution.py:30
  48.6 4.6 %collective-permute-start.2 = (bf16[520,336]{1,0:T(8,128)(2,1)S(1)}, bf16[520,336]{1,0:T(8,128)(2,1)S(1)}, u32[]{:S(2)}, u32[]{:S(2)}) collective-permute-start(bf16[520,336]{1,0:T(8,128)(2,1)S(1)} %collective-permute-done.1), channel_id=1, source_target_pairs={{0,14},{2,0},{4,2},{6,4},{8,6},{10,8},{12,10},{14,12},{1,15},{3,1}... | collective-permute-start | bytes 1048328 | tf_op jit(solution)/shard_map/ppermute | solution.py:33
  53.2 5.2 %collective-permute-done.5 = bf16[520,336]{1,0:T(8,128)(2,1)S(1)} collective-permute-done((bf16[520,336]{1,0:T(8,128)(2,1)S(1)}, bf16[520,336]{1,0:T(8,128)(2,1)S(1)}, u32[]{:S(2)}, u32[]{:S(2)}) %collective-permute-start.5) | collective-permute-done | bytes 349472 | tf_op jit(solution)/shard_map/ppermute | solution.py:30
  60.3 8.9 %collective-permute-done.6 = bf16[520,336]{1,0:T(8,128)(2,1)S(1)} collective-permute-done((bf16[520,336]{1,0:T(8,128)(2,1)S(1)}, bf16[520,336]{1,0:T(8,128)(2,1)S(1)}, u32[]{:S(2)}, u32[]{:S(2)}) %collective-permute-start.6) | collective-permute-done | bytes 349472 | tf_op jit(solution)/shard_map/ppermute | solution.py:30
  69.3 7.6 %concatenate.44 = bf16[520,5376]{1,0:T(8,128)(2,1)} concatenate(bf16[520,336]{1,0:T(8,128)(2,1)S(1)} %concatenate.43, bf16[520,336]{1,0:T(8,128)(2,1)S(1)} %collective-permute-done, bf16[520,336]{1,0:T(8,128)(2,1)S(1)} %collective-permute-done.1, bf16[520,336]{1,0:T(8,128)(2,1)S(1)} %collective-permute-done.2, bf16[520,336]{1,0:T(8,128)(2,1)S(1)} %collective-permute-done.6, ...), dimensions={1} | concatenate | bytes 11182080 | tf_op jit(solution)/shard_map/concatenate | solution.py:39
  76.8 3.3 %constant_dynamic-slice_fusion = bf16[520,2688]{1,0:T(8,128)(2,1)S(1)} fusion(bf16[520,5376]{1,0:T(8,128)(2,1)} %concatenate.44, s32[]{:T(128)S(6)} %select_n.22), kind=kLoop, calls=%fused_computation.80 | loop fusion | bytes 5591044 | tf_op jit(solution)/shard_map/dynamic_slice | solution.py:41
  80.1 6.0 %collective-permute-start.7 = (bf16[520,2688]{1,0:T(8,128)(2,1)S(1)}, bf16[520,2688]{1,0:T(8,128)(2,1)}, u32[]{:S(2)}, u32[]{:S(2)}) collective-permute-start(bf16[520,2688]{1,0:T(8,128)(2,1)S(1)} %constant_dynamic-slice_fusion), channel_id=1, source_target_pairs={{0,1},{1,0},{2,3},{3,2},{4,5},{5,4},{6,7},{7,6},{8,9},{9,8},{10,11... | collective-permute-start | bytes 8386568 | tf_op jit(solution)/shard_map/ppermute | solution.py:30
  87.9 2.0 %fusion.16 = pred[512,1536]{0,1:T(8,128)(4,1)} fusion(s32[1536]{0:T(1024)S(1)} %iota_add_fusion, s32[512]{0:T(512)S(1)} %iota_add_fusion.1, pred[1536]{0:T(1024)(128)(4,1)S(1)} %broadcast_compare_fusion), kind=kLoop, calls=%fused_computation.28 | loop fusion | flops 3932160 | bytes 796160 | tf_op jit(solution)/shard_map/and | solution.py:151
  90.8 5.2 %fusion.5 = bf16[520,5376]{1,0:T(8,128)(2,1)S(1)} fusion(s32[]{:T(128)S(6)} %select_n.24, bf16[520,2688]{1,0:T(8,128)(2,1)S(1)} %constant_dynamic-slice_fusion, bf16[520,2688]{1,0:T(8,128)(2,1)} %collective-permute-done.7), kind=kLoop, calls=%fused_computation.13 | loop fusion | flops 22364160 | bytes 11182084 | tf_op jit(solution)/shard_map/concatenate | solution.py:39
  96.1 2.3 %copy-done = bf16[520,5376]{1,0:T(8,128)(2,1)} copy-done((bf16[520,5376]{1,0:T(8,128)(2,1)}, bf16[520,5376]{1,0:T(8,128)(2,1)S(1)}, u32[]{:S(2)}) %copy-start) | copy-done | bytes 5591064
  99.6 46.8 %all-to-all-done = bf16[32,176,512]{2,1,0:T(8,128)(2,1)} async-done(((bf16[32,176,512]{2,1,0:T(8,128)(2,1)}), bf16[32,176,512]{2,1,0:T(8,128)(2,1)}, u32[]{:S(2)}, u32[]{:S(2)}) %all-to-all-start) | async-done | bytes 5767200 | tf_op jit(solution)/shard_map/all_to_all | solution.py:88
  147.4 3.2 %fusion.47 = (bf16[32,168,256]{2,1,0:T(8,128)(2,1)S(1)}, bf16[32,168,256]{2,1,0:T(8,128)(2,1)S(1)}) fusion(bf16[32,176,512]{2,1,0:T(8,128)(2,1)} %all-to-all-done), kind=kLoop, calls=%fused_computation.90 | loop fusion | bytes 11010048 | tf_op jit(solution)/shard_map/slice | solution.py:93
  152.1 2.0 %fusion.23 = f32[512,256]{0,1:T(8,128)S(1)} fusion(bf16[5376,256]{1,0:T(8,128)(2,1)S(1)} %bitcast.65, f32[5376]{0:T(1024)S(1)} %fusion.39, f32[512]{0:T(512)S(1)} %add_rsqrt_fusion.2, bf16[520,5376]{1,0:T(8,128)(2,1)S(1)} %bitcast.60), kind=kOutput, calls=%fused_computation.32 | convolution fusion | flops 1420296192 | bytes 8808448 | tf_op jit(solution)/shard_map/dot_general | solution.py:122
  154.9 7.1 %collective-permute-start.8 = (bf16[512,2,128]{0,2,1:T(8,128)(2,1)S(1)}, bf16[512,2,128]{0,2,1:T(8,128)(2,1)}, u32[]{:S(2)}, u32[]{:S(2)}) collective-permute-start(bf16[512,2,128]{0,2,1:T(8,128)(2,1)S(1)} %pad_maximum_fusion), channel_id=1, source_target_pairs={{0,32},{16,48},{32,64},{48,80},{64,96},{80,112},{96,128},{112,144}... | collective-permute-start | bytes 786440 | tf_op jit(solution)/shard_map/ppermute | solution.py:19
  161.9 6.7 %collective-permute-start.9 = (bf16[512,2,128]{0,2,1:T(8,128)(2,1)S(1)}, bf16[512,2,128]{0,2,1:T(8,128)(2,1)}, u32[]{:S(2)}, u32[]{:S(2)}) collective-permute-start(bf16[512,2,128]{0,2,1:T(8,128)(2,1)S(1)} %pad_maximum_fusion), channel_id=1, source_target_pairs={{0,16},{16,32},{32,48},{48,64},{64,80},{80,96},{96,112},{112,128},... | collective-permute-start | bytes 786440 | tf_op jit(solution)/shard_map/ppermute | solution.py:19
  168.8 3.0 %copy.46 = bf16[256,5376]{1,0:T(8,128)(2,1)} copy(bf16[256,5376]{0,1:T(8,128)(2,1)S(1)} %bitcast.63) | data formatting | bytes 5505024 | tf_op jit(solution)/shard_map/dot_general | solution.py:125
  171.8 5.2 %multiply_reduce_fusion = (f32[512,2]{0,1:T(2,128)S(1)}, f32[512,2,128]{0,2,1:T(8,128)S(1)}) fusion(bf16[2,128,5376]{2,1,0:T(8,128)(2,1)} %bitcast.64, f32[5376]{0:T(1024)} %copy-done.3, f32[512]{0:T(512)S(1)} %add_rsqrt_fusion.2, bf16[520,5376]{1,0:T(8,128)(2,1)} %copy-done), kind=kOutput, calls=%fused_computation.35 | convolution fusion | flops 1420557312 | bytes 8812544 | tf_op jit(solution)/shard_map/dot_general | solution.py:125
  180.0 2.0 %fusion.19 = bf16[128,2,512]{2,0,1:T(8,128)(2,1)S(1)} fusion(f32[2,512]{1,0:T(2,128)S(1)} %get-tuple-element.22, f32[1536,512,2]{1,0,2:T(8,128)S(1)} %get-tuple-element.23, pred[512,1536]{0,1:T(8,128)(4,1)S(1)} %copy-done.1, bf16[1536,2,128]{0,2,1:T(8,128)(2,1)S(1)} %maximum_maximum_fusion), kind=kOutput, calls=%fused_computation.31 | convolution fusion | flops 409075712 | bytes 7737344 | tf_op jit(solution)/shard_map/kgts,skd->tkgd/dot_general | solution.py:155
  (71 shorter events, 19.5 us)
Async XLA Ops:
  5.8 14.0 %copy-start.4 = (f32[336]{0:T(512)S(1)}, f32[336]{0:T(512)}, u32[]{:S(2)}) copy-start(f32[336]{0:T(512)} %param.8) | copy-start | bytes 4036
  5.9 14.0 %copy-start.2 = (bf16[512,336]{0,1:T(8,128)(2,1)S(1)}, bf16[512,336]{0,1:T(8,128)(2,1)}, u32[]{:S(2)}) copy-start(bf16[512,336]{0,1:T(8,128)(2,1)} %param.7) | copy-start | bytes 1032196
  5.9 140.5 %all-to-all-start = ((bf16[32,176,512]{2,1,0:T(8,128)(2,1)}), bf16[32,176,512]{2,1,0:T(8,128)(2,1)}, u32[]{:S(2)}, u32[]{:S(2)}) async-start(bf16[32,176,512]{2,1,0:T(8,128)(2,1)} %stack.2), calls=%async_computation | async-start | bytes 11534336 | tf_op jit(solution)/shard_map/all_to_all | solution.py:88
  20.4 13.8 %collective-permute-start.3 = (bf16[520,336]{1,0:T(8,128)(2,1)S(1)}, bf16[520,336]{1,0:T(8,128)(2,1)S(1)}, u32[]{:S(2)}, u32[]{:S(2)}) collective-permute-start(bf16[520,336]{1,0:T(8,128)(2,1)S(1)} %concatenate.43), channel_id=1, source_target_pairs={{0,2},{2,4},{4,6},{6,8},{8,10},{10,12},{12,14},{14,0},{1,3},{3,5},... | collective-permute-start | bytes 1048328 | tf_op jit(solution)/shard_map/ppermute | solution.py:30
  23.6 12.6 %collective-permute-start = (bf16[520,336]{1,0:T(8,128)(2,1)S(1)}, bf16[520,336]{1,0:T(8,128)(2,1)S(1)}, u32[]{:S(2)}, u32[]{:S(2)}) collective-permute-start(bf16[520,336]{1,0:T(8,128)(2,1)S(1)} %concatenate.43), channel_id=1, source_target_pairs={{0,14},{2,0},{4,2},{6,4},{8,6},{10,8},{12,10},{14,12},{1,15},{3,1}... | collective-permute-start | bytes 1048328 | tf_op jit(solution)/shard_map/ppermute | solution.py:33
  34.2 12.5 %collective-permute-start.4 = (bf16[520,336]{1,0:T(8,128)(2,1)S(1)}, bf16[520,336]{1,0:T(8,128)(2,1)S(1)}, u32[]{:S(2)}, u32[]{:S(2)}) collective-permute-start(bf16[520,336]{1,0:T(8,128)(2,1)S(1)} %collective-permute-done.3), channel_id=1, source_target_pairs={{0,2},{2,4},{4,6},{6,8},{8,10},{10,12},{12,14},{14,0},{1,3},{3,5},... | collective-permute-start | bytes 1048328 | tf_op jit(solution)/shard_map/ppermute | solution.py:30
  36.2 12.5 %collective-permute-start.1 = (bf16[520,336]{1,0:T(8,128)(2,1)S(1)}, bf16[520,336]{1,0:T(8,128)(2,1)S(1)}, u32[]{:S(2)}, u32[]{:S(2)}) collective-permute-start(bf16[520,336]{1,0:T(8,128)(2,1)S(1)} %collective-permute-done), channel_id=1, source_target_pairs={{0,14},{2,0},{4,2},{6,4},{8,6},{10,8},{12,10},{14,12},{1,15},{3,1}... | collective-permute-start | bytes 1048328 | tf_op jit(solution)/shard_map/ppermute | solution.py:33
  46.7 11.7 %collective-permute-start.5 = (bf16[520,336]{1,0:T(8,128)(2,1)S(1)}, bf16[520,336]{1,0:T(8,128)(2,1)S(1)}, u32[]{:S(2)}, u32[]{:S(2)}) collective-permute-start(bf16[520,336]{1,0:T(8,128)(2,1)S(1)} %collective-permute-done.4), channel_id=1, source_target_pairs={{0,2},{2,4},{4,6},{6,8},{8,10},{10,12},{12,14},{14,0},{1,3},{3,5},... | collective-permute-start | bytes 1048328 | tf_op jit(solution)/shard_map/ppermute | solution.py:30
  48.6 11.7 %collective-permute-start.2 = (bf16[520,336]{1,0:T(8,128)(2,1)S(1)}, bf16[520,336]{1,0:T(8,128)(2,1)S(1)}, u32[]{:S(2)}, u32[]{:S(2)}) collective-permute-start(bf16[520,336]{1,0:T(8,128)(2,1)S(1)} %collective-permute-done.1), channel_id=1, source_target_pairs={{0,14},{2,0},{4,2},{6,4},{8,6},{10,8},{12,10},{14,12},{1,15},{3,1}... | collective-permute-start | bytes 1048328 | tf_op jit(solution)/shard_map/ppermute | solution.py:33
  58.4 10.9 %collective-permute-start.6 = (bf16[520,336]{1,0:T(8,128)(2,1)S(1)}, bf16[520,336]{1,0:T(8,128)(2,1)S(1)}, u32[]{:S(2)}, u32[]{:S(2)}) collective-permute-start(bf16[520,336]{1,0:T(8,128)(2,1)S(1)} %collective-permute-done.5), channel_id=1, source_target_pairs={{0,2},{2,4},{4,6},{6,8},{8,10},{10,12},{12,14},{14,0},{1,3},{3,5},... | collective-permute-start | bytes 1048328 | tf_op jit(solution)/shard_map/ppermute | solution.py:30
  80.1 10.7 %collective-permute-start.7 = (bf16[520,2688]{1,0:T(8,128)(2,1)S(1)}, bf16[520,2688]{1,0:T(8,128)(2,1)}, u32[]{:S(2)}, u32[]{:S(2)}) collective-permute-start(bf16[520,2688]{1,0:T(8,128)(2,1)S(1)} %constant_dynamic-slice_fusion), channel_id=1, source_target_pairs={{0,1},{1,0},{2,3},{3,2},{4,5},{5,4},{6,7},{7,6},{8,9},{9,8},{10,11... | collective-permute-start | bytes 8386568 | tf_op jit(solution)/shard_map/ppermute | solution.py:30
  96.0 2.4 %copy-start = (bf16[520,5376]{1,0:T(8,128)(2,1)}, bf16[520,5376]{1,0:T(8,128)(2,1)S(1)}, u32[]{:S(2)}) copy-start(bf16[520,5376]{1,0:T(8,128)(2,1)S(1)} %fusion.5) | copy-start | bytes 16773124
  98.4 53.6 %copy-start.3 = (f32[5376]{0:T(1024)}, f32[5376]{0:T(1024)S(1)}, u32[]{:S(2)}) copy-start(f32[5376]{0:T(1024)S(1)} %fusion.39) | copy-start | bytes 64516
  147.4 4.6 %slice-start = ((s8[5591040]{0:T(1024)(128)(4,1)}), s8[4194304]{0:T(1024)(128)(4,1)S(1)}, s32[]{:S(2)}) async-start(s8[5591040]{0:T(1024)(128)(4,1)} %bitcast.59), calls=%async_computation.1 | async-start | bytes 8388608
  150.5 1.5 slice-start.1
  152.1 2.1 %copy-start.5 = (f32[128]{0:T(128)S(1)}, f32[128]{0:T(128)}, u32[]{:S(2)}) copy-start(f32[128]{0:T(128)} %param.10) | copy-start | bytes 1540
  154.9 22.4 %collective-permute-start.8 = (bf16[512,2,128]{0,2,1:T(8,128)(2,1)S(1)}, bf16[512,2,128]{0,2,1:T(8,128)(2,1)}, u32[]{:S(2)}, u32[]{:S(2)}) collective-permute-start(bf16[512,2,128]{0,2,1:T(8,128)(2,1)S(1)} %pad_maximum_fusion), channel_id=1, source_target_pairs={{0,32},{16,48},{32,64},{48,80},{64,96},{80,112},{96,128},{112,144}... | collective-permute-start | bytes 786440 | tf_op jit(solution)/shard_map/ppermute | solution.py:19
  161.9 15.3 %collective-permute-start.9 = (bf16[512,2,128]{0,2,1:T(8,128)(2,1)S(1)}, bf16[512,2,128]{0,2,1:T(8,128)(2,1)}, u32[]{:S(2)}, u32[]{:S(2)}) collective-permute-start(bf16[512,2,128]{0,2,1:T(8,128)(2,1)S(1)} %pad_maximum_fusion), channel_id=1, source_target_pairs={{0,16},{16,32},{32,48},{48,64},{64,80},{80,96},{96,112},{112,128},... | collective-permute-start | bytes 786440 | tf_op jit(solution)/shard_map/ppermute | solution.py:19
  171.8 5.2 %copy-start.6 = (f32[128]{0:T(128)S(1)}, f32[128]{0:T(128)}, u32[]{:S(2)}) copy-start(f32[128]{0:T(128)} %param.9) | copy-start | bytes 1540
  171.8 6.5 %copy-start.1 = (pred[512,1536]{0,1:T(8,128)(4,1)S(1)}, pred[512,1536]{0,1:T(8,128)(4,1)}, u32[]{:S(2)}) copy-start(pred[512,1536]{0,1:T(8,128)(4,1)} %fusion.16) | copy-start | bytes 2359300
